TPU v7x, 512 devices: a whole 4x8x8 slice. The times are simulated.
512 devices in a mesh: req: 64 (over x, y, core), tp: 8 (over z).
Axes of the slice: x: 4, y: 8, z: 8, core: 2. Of those that a mesh axis runs over, the one named last changes fastest.
Arguments:
- vit_context: bfloat16 [32768, 4096], P('req', 'tp'), may hold values from -6 to 6
- vision_residual: bfloat16 [32768, 4096], P('req', 'tp'), may hold values from -75 to 75
- out_weight: bfloat16 [4096, 4096], P('tp', 'req'), may hold values from -0.09375 to 0.09375
- layer_scale: float32 [4096], P('tp'), may hold values from 0.2 to 2
- prompt: bfloat16 [64, 256, 4096], P('req', None, 'tp'), may hold values from -75 to 75
- prompt_len: int32 [64], P('req'), may hold values from 128 to 256
- image_at: int32 [64], P('req'), may hold values from 0 to 128
- grid_sizes: int32 [128, 2], replicated, may hold values from 7 to 8, as said below
- image_owner: int32 [128], replicated, may hold values from 0 to 63, as said below
- norm_gain: float32 [4096], replicated, may hold values from 0.5 to 1.5
- qkv_weight: bfloat16 [4096, 6144], P('req', 'tp'), may hold values from -0.09375 to 0.09375
Outputs:
- qkv: bfloat16 [24576, 6144], P('req', 'tp')
Inputs may be any that keep to these rules, and one draw needn't show every extreme that they name: `image_owner`: each request owns exactly 2 images. `grid_sizes`: each side is 7 or 8; in every draw the images of some request are all 8 by 8, so that request has exactly 128 merged rows.
All inputs are finite; a program needn't handle non-finite values.
Results may differ from a plain program's by a relative error of at most 0.008.
Values may be sent and summed in bfloat16 or wider, within the bound.
No kernel may reach another device: no remote copies, remote signals or barrier semaphores. Data moves between devices by JAX's collectives and lax.ppermute only.
A program may use at most 64 MiB of HBM per device.

v0:
```python
import jax
import jax.numpy as jnp
from jax import lax
from jax.sharding import PartitionSpec as P

HEAD = 128
GROUP = 4
IMG_MAX = 128


def request_plan(grid_sizes, image_owner, requests):
    image_rows = grid_sizes[:, 0] * grid_sizes[:, 1]
    member = (image_owner[:, None] == jnp.arange(requests, dtype=jnp.int32)[None, :]).astype(
        jnp.int32
    )
    counts = jnp.sum(image_rows[:, None] * member, axis=0)
    starts = jnp.cumsum(counts) - counts
    return (counts, starts)


def rope_tables(count):
    half_size = HEAD // 2
    exponent = jnp.arange(half_size, dtype=jnp.float32) * (2.0 / HEAD)
    frequency = jnp.exp(-exponent * jnp.log(jnp.float32(500000.0)))
    angles = jnp.arange(count, dtype=jnp.float32)[:, None] * frequency[None, :]
    return (jnp.cos(angles), jnp.sin(angles))


def apply_rope(projected, cosine_table, sine_table):
    seq_rows = projected.shape[0]
    head_blocks = projected.reshape(seq_rows, -1, GROUP + 2, HEAD)
    turning = head_blocks[:, :, : GROUP + 1, :]
    first_half = turning[..., : HEAD // 2]
    second_half = turning[..., HEAD // 2 :]
    cosine_wide = cosine_table[:, None, None, :]
    sine_wide = sine_table[:, None, None, :]
    turned = jnp.concatenate(
        [
            first_half * cosine_wide - second_half * sine_wide,
            second_half * cosine_wide + first_half * sine_wide,
        ],
        axis=-1,
    )
    head_blocks = jnp.concatenate([turned, head_blocks[:, :, GROUP + 1 :, :]], axis=2)
    return head_blocks.reshape(seq_rows, -1)


def normalize(embedded, norm_gain):
    values = embedded.astype(jnp.float32)
    mean_square = jnp.mean(values * values, axis=-1, keepdims=True)
    return (values * lax.rsqrt(mean_square + 1e-05) * norm_gain[None, :]).astype(jnp.bfloat16)


def shards(
    vit_context,
    vision_residual,
    out_weight,
    layer_scale,
    prompt,
    prompt_len,
    image_at,
    grid_sizes,
    image_owner,
    norm_gain,
    qkv_weight,
):
    requests = lax.axis_size("req")
    device_index = lax.axis_index("req")
    feature_width = vit_context.shape[1]
    merged_context = jnp.mean(
        vit_context.astype(jnp.float32).reshape(-1, 4, feature_width), axis=1
    ).astype(jnp.bfloat16)
    merged_residual = jnp.mean(
        vision_residual.astype(jnp.float32).reshape(-1, 4, feature_width), axis=1
    )
    partial_value = jnp.dot(
        merged_context,
        lax.all_gather(out_weight, "req", axis=1, tiled=True),
        preferred_element_type=jnp.float32,
    )
    summed = lax.psum(partial_value.astype(jnp.bfloat16), "tp").astype(jnp.float32)
    own_share = lax.dynamic_slice_in_dim(
        summed, lax.axis_index("tp") * feature_width, feature_width, 1
    )
    merged = (merged_residual + layer_scale[None, :] * own_share).astype(jnp.bfloat16)
    merged_count = merged.shape[0]
    counts, starts = request_plan(grid_sizes, image_owner, requests)
    request_ends = starts + counts
    capacity = (IMG_MAX + requests - 1) // requests
    request_ids = jnp.arange(requests, dtype=jnp.int32)
    group_index = jnp.arange(merged_count, dtype=jnp.int32) * requests + device_index
    destination = jnp.sum((request_ends[None, :] <= group_index[:, None]).astype(jnp.int32), axis=1)
    owned_start = jnp.sum(
        jnp.where(destination[:, None] == request_ids[None, :], starts[None, :], 0), axis=1
    )
    target = destination * capacity + (group_index - owned_start) // requests
    usable = destination < requests
    send_slots = jnp.arange(requests * capacity, dtype=jnp.int32)
    placing = ((send_slots[:, None] == target[None, :]) & usable[None, :]).astype(jnp.bfloat16)
    outgoing = jnp.dot(placing, merged, preferred_element_type=jnp.float32).astype(jnp.bfloat16)
    arrived = lax.all_to_all(
        outgoing.reshape(requests, capacity, feature_width),
        "req",
        split_axis=0,
        concat_axis=0,
        tiled=True,
    )
    arrived = arrived.reshape(requests * capacity, feature_width)
    own_request = request_ids == device_index
    own_count = jnp.sum(jnp.where(own_request, counts, 0))
    own_start = jnp.sum(jnp.where(own_request, starts, 0))
    image_from = image_at[0]
    prompt_count = prompt_len[0]
    seq_slots = prompt.shape[1] + IMG_MAX
    slot_index = jnp.arange(seq_slots, dtype=jnp.int32)
    image_row = slot_index - image_from
    in_image = (image_row >= 0) & (image_row < own_count)
    is_live = slot_index < prompt_count + own_count
    from_prompt = is_live & jnp.logical_not(in_image)
    flat_index = (own_start + image_row) % requests * capacity + image_row // requests
    image_pick = ((flat_index[:, None] == send_slots[None, :]) & in_image[:, None]).astype(
        jnp.bfloat16
    )
    prompt_row = jnp.where(slot_index < image_from, slot_index, slot_index - own_count)
    prompt_ids = jnp.arange(prompt.shape[1], dtype=jnp.int32)
    prompt_pick = ((prompt_row[:, None] == prompt_ids[None, :]) & from_prompt[:, None]).astype(
        jnp.bfloat16
    )
    embedded = (
        jnp.dot(image_pick, arrived, preferred_element_type=jnp.float32)
        + jnp.dot(prompt_pick, prompt[0], preferred_element_type=jnp.float32)
    ).astype(jnp.bfloat16)
    gathered = lax.all_gather(embedded, "tp", axis=1, tiled=True)
    normed = normalize(gathered, norm_gain)
    projected = jnp.dot(
        normed,
        lax.all_gather(qkv_weight, "req", axis=0, tiled=True),
        preferred_element_type=jnp.float32,
    )
    cosine_table, sine_table = rope_tables(seq_slots)
    return apply_rope(projected, cosine_table, sine_table).astype(jnp.bfloat16)


def solution(mesh):
    in_specs = (
        P("req", "tp"),
        P("req", "tp"),
        P("tp", "req"),
        P("tp"),
        P("req", None, "tp"),
        P("req"),
        P("req"),
        P(),
        P(),
        P(),
        P("req", "tp"),
    )
    out_specs = P("req", "tp")
    return jax.shard_map(shards, mesh=mesh, in_specs=in_specs, out_specs=out_specs, check_vma=False)
```

profile of v0, /device:TPU:1, one launch (start us, length us, event | category | flops | bytes accessed | tf_op | source)
XLA Modules:
  0.0 352.9 jit_solution(7770393168710454331)
XLA Ops:
  6.5 0.7 all-gather.4.cloned.1.call-update
  7.3 1.4 reshape.205
  8.7 0.6 reduce_sum.78
  9.3 0.8 multiply_bitcast_fusion
  10.1 91.0 %all-gather.4.cloned.1.call-done = bf16[512,4096]{0,1:T(8,128)(2,1)} async-done(((bf16[512,64]{0,1:T(8,128)(2,1)}), bf16[512,4096]{0,1:T(8,128)(2,1)}) %all-gather.4.cloned.1.call-update) | async-done | bytes 4194320 | tf_op jit(solution)/shard_map/all_gather | solution.py:78
  101.1 4.6 %convolution_convert_fusion = bf16[128,4096]{1,0:T(8,128)(2,1)} fusion(bf16[512,4096]{0,1:T(8,128)(2,1)} %all-gather.4.cloned.1.call-done, f32[128,512]{1,0:T(8,128)S(1)} %reduce_sum.78), kind=kOutput, calls=%fused_computation.5 | convolution fusion | flops 537526272 | bytes 5505024 | tf_op jit(solution)/shard_map/dot_general | solution.py:76
  105.7 0.1 select_reduce_fusion.1
  105.8 0.1 copy.16
  105.9 0.1 reduce-window.7
  106.0 0.1 reduce
  106.2 0.3 reshape.203
  106.5 0.6 reduce_sum.77
  107.2 0.1 convert_reduce_fusion
  107.3 0.7 fusion.38
  108.0 0.1 select_reduce_fusion
  108.1 73.3 %all-reduce.2.cloned.1.call-done = bf16[128,4096]{1,0:T(8,128)(2,1)} async-done(((bf16[128,4096]{1,0:T(8,128)(2,1)}), bf16[128,4096]{1,0:T(8,128)(2,1)}) %all-reduce.2.cloned.1.call-update) | async-done | bytes 1048592 | tf_op jit(solution)/shard_map/psum | solution.py:81
  181.4 1.1 convolution_convert_fusion.1
  182.5 0.7 reshape.199
  183.3 14.2 %all-to-all-start = ((bf16[64,2,512]{2,1,0:T(2,128)(2,1)}), bf16[64,2,512]{2,1,0:T(2,128)(2,1)S(1)}, u32[]{:S(2)}, u32[]{:S(2)}) async-start(bf16[64,2,512]{2,1,0:T(2,128)(2,1)} %reshape.199), calls=%async_computation | async-start | bytes 262144 | tf_op jit(solution)/shard_map/all_to_all | solution.py:101
  199.3 0.6 fusion.37
  199.9 1.3 fusion.30
  201.2 6.6 %all-to-all-done = bf16[64,2,512]{2,1,0:T(2,128)(2,1)S(1)} async-done(((bf16[64,2,512]{2,1,0:T(2,128)(2,1)}), bf16[64,2,512]{2,1,0:T(2,128)(2,1)S(1)}, u32[]{:S(2)}, u32[]{:S(2)}) %all-to-all-start) | async-done | bytes 131104 | tf_op jit(solution)/shard_map/all_to_all | solution.py:101
  207.9 0.3 fusion.14
  208.2 1.1 fusion.7
  209.3 0.5 all-gather.8.cloned.1.call-update
  209.9 0.4 fusion.21
  210.3 40.0 %all-gather.6.cloned.1.call-done = bf16[384,4096]{1,0:T(8,128)(2,1)} async-done(((bf16[384,512]{1,0:T(8,128)(2,1)}), bf16[384,4096]{1,0:T(8,128)(2,1)}) %all-gather.6.cloned.1.call-update) | async-done | bytes 3145744 | tf_op jit(solution)/shard_map/all_gather | solution.py:133
  250.3 2.6 fusion
  252.9 85.4 %all-gather.8.cloned.1.call-done = bf16[4096,768]{1,0:T(8,128)(2,1)} async-done(((bf16[64,768]{1,0:T(8,128)(2,1)}), bf16[4096,768]{1,0:T(8,128)(2,1)}) %all-gather.8.cloned.1.call-update) | async-done | bytes 6291472 | tf_op jit(solution)/shard_map/all_gather | solution.py:137
  338.3 6.7 %fusion.3 = f32[384,768]{0,1:T(8,128)S(1)} fusion(bf16[4096,768]{1,0:T(8,128)(2,1)} %all-gather.8.cloned.1.call-done, bf16[384,4096]{1,0:T(8,128)(2,1)} %all-gather.6.cloned.1.call-done, f32[4096]{0:T(1024)S(1)} %copy-done.3, f32[384]{0:T(512)S(1)} %add_rsqrt_fusion), kind=kOutput, calls=%fused_computation.6 | convolution fusion | flops 2422210560 | bytes 10634752 | tf_op jit(solution)/shard_map/dot_general | solution.py:135
  345.0 0.1 subtract_convert_fusion
  345.2 1.1 copy.18
  (24 shorter events, 0.4 us)
Async XLA Ops:
  6.5 201.7 %copy-start = (bf16[1,256,512]{2,1,0:T(8,128)(2,1)S(1)}, bf16[1,256,512]{2,1,0:T(8,128)(2,1)}, u32[]{:S(2)}) copy-start(bf16[1,256,512]{2,1,0:T(8,128)(2,1)} %param.15) | copy-start | bytes 786436
  6.5 94.5 %all-gather.4.cloned.1.call-start = ((), (), s32[]{:S(2)}) async-start(), calls=%async_computation.1 | async-start | bytes 4259840 | tf_op jit(solution)/shard_map/all_gather | solution.py:78
  7.3 174.2 %all-reduce.2.cloned.1.call-start = ((), (), s32[]{:S(2)}) async-start(), calls=%async_computation.2 | async-start | bytes 2097152 | tf_op jit(solution)/shard_map/psum | solution.py:81
  8.7 97.0 %copy-start.4 = (s32[128]{0:T(128)S(1)}, s32[128]{0:T(128)}, u32[]{:S(2)}) copy-start(s32[128]{0:T(128)} %param.19) | copy-start | bytes 1540
  8.7 97.5 %copy-start.1 = (bf16[512,512]{1,0:T(8,128)(2,1)S(1)}, bf16[512,512]{1,0:T(8,128)(2,1)}, u32[]{:S(2)}) copy-start(bf16[512,512]{1,0:T(8,128)(2,1)} %param.12) | copy-start | bytes 1572868
  10.1 171.3 %copy-start.2 = (f32[512]{0:T(512)S(1)}, f32[512]{0:T(512)}, u32[]{:S(2)}) copy-start(f32[512]{0:T(512)} %param.14) | copy-start | bytes 6148
  106.5 231.8 %copy-start.3 = (f32[4096]{0:T(1024)S(1)}, f32[4096]{0:T(1024)}, u32[]{:S(2)}) copy-start(f32[4096]{0:T(1024)} %param.20) | copy-start | bytes 49156
  183.3 24.5 %all-to-all-start = ((bf16[64,2,512]{2,1,0:T(2,128)(2,1)}), bf16[64,2,512]{2,1,0:T(2,128)(2,1)S(1)}, u32[]{:S(2)}, u32[]{:S(2)}) async-start(bf16[64,2,512]{2,1,0:T(2,128)(2,1)} %reshape.199), calls=%async_computation | async-start | bytes 262144 | tf_op jit(solution)/shard_map/all_to_all | solution.py:101
  197.4 52.9 %all-gather.6.cloned.1.call-start = ((), (), s32[]{:S(2)}) async-start(), calls=%async_computation.3 | async-start | bytes 3538944 | tf_op jit(solution)/shard_map/all_gather | solution.py:133
  209.3 129.0 %all-gather.8.cloned.1.call-start = ((), (), s32[]{:S(2)}) async-start(), calls=%async_computation.4 | async-start | bytes 6389760 | tf_op jit(solution)/shard_map/all_gather | solution.py:137
Sparse Core Ops, SparseCore 0:
  10.7 90.2 all-gather.3
  105.8 75.5 all-reduce.1
  209.4 40.8 all-gather.5
  253.5 84.7 all-gather.7
where the time goes:
time: 353 us
  waiting for transfers between devices  298 us (84%)
  between operations  15.2 us (4%)
  starting transfers between devices  14.3 us (4%)
  matrix products  13.8 us (4%)
  other arithmetic  8.27 us (2%)
  local copies, waits for them, and re-layouts  3.69 us (1%)
    all_gather x1, waiting for transfers between devices, shards(): lax.all_gather(out_weight, 'req', axis=1, tiled=True)  91 us
    all_gather x1, waiting for transfers between devices, shards(): lax.all_gather(qkv_weight, 'req', axis=0, tiled=True)  85.4 us
    psum x1, waiting for transfers between devices, shards(): lax.psum(partial_value.astype(jnp.bfloat16), 'tp').astype(jnp.float32)  73.3 us
    all_gather x1, waiting for transfers between devices, shards(): gathered = lax.all_gather(embedded, 'tp', axis=1, tiled=True)  40 us
    all_to_all x1, starting transfers between devices, shards(): lax.all_to_all(outgoing.reshape(requests, capacity, feature_width), 'req'...  14.2 us
  transfers between devices with their start and end apart: 5, of which 5 were waited for; matrix products, arithmetic and copies ran while one was open for 3% of the time, Pallas kernels for 0%

commit v1 on v0

--- a/solution.py
+++ b/solution.py
@@ -1,3 +1,4 @@
+import functools
 import jax
 import jax.numpy as jnp
 from jax import lax
@@ -6,6 +7,24 @@
 HEAD = 128
 GROUP = 4
 IMG_MAX = 128
+
+
+def tracks_serve(inp, comm_axis):
+    chips = lax.axis_size(comm_axis)
+    kept_rows = tuple(((ix, (ix + 1) % chips) for ix in range(chips)))
+    all_blocks = tuple(((ix, (ix - 1) % chips) for ix in range(chips)))
+    y_new, new = ([inp], [inp])
+    for _ in range(chips // 2):
+        wide_out = lax.ppermute(y_new[-1], comm_axis, kept_rows)
+        y_new.append(wide_out)
+    for _ in [*range((chips - 1) // 2)]:
+        q_next = lax.ppermute(new[-1], comm_axis, all_blocks)
+        new.append(q_next)
+    formed = jnp.concatenate([*y_new[::-1], *new[1:]], axis=1)
+    return jnp.roll(formed, shift=(lax.axis_index(comm_axis) - chips // 2) * inp.shape[1], axis=1)
+
+
+draw_the_pages = functools.partial(tracks_serve, comm_axis="tp")
 
 
 def request_plan(grid_sizes, image_owner, requests):
@@ -130,7 +149,7 @@
         jnp.dot(image_pick, arrived, preferred_element_type=jnp.float32)
         + jnp.dot(prompt_pick, prompt[0], preferred_element_type=jnp.float32)
     ).astype(jnp.bfloat16)
-    gathered = lax.all_gather(embedded, "tp", axis=1, tiled=True)
+    gathered = draw_the_pages(embedded)
     normed = normalize(gathered, norm_gain)
     projected = jnp.dot(
         normed,

time: 353 us -> 288 us (0.82)
  waiting for transfers between devices: 298 us -> 210 us
  starting transfers between devices: 14.3 us -> 36.4 us
    all_gather x1, waiting for transfers between devices: 85.4 us -> 10.8 us  [shards(): lax.all_gather(qkv_weight, 'req', axis=0, tiled=True)]
    all_gather x1 -> x0, waiting for transfers between devices: 40 us -> none  [shards(): gathered = lax.all_gather(embedded, 'tp', axis=1, tiled=True)]
    ppermute x0 -> x7, waiting for transfers between devices: none -> 27.1 us  [the longest x4 26.1 us: tracks_serve(): wide_out = lax.ppermute(y_new[-1], comm_axis, kept_rows)]
    ppermute x0 -> x7, starting transfers between devices: none -> 22.1 us  [the longest x3 13.7 us: tracks_serve(): q_next = lax.ppermute(new[-1], comm_axis, all_blocks)]
  transfers between devices with their start and end apart: 5 -> 11, of which waited for: 5 -> 9; matrix products, arithmetic and copies ran while one was open for 3% -> 4% of each run, Pallas kernels for 0% -> 0%
where the time goes in v1:
time: 288 us
  waiting for transfers between devices  210 us (73%)
  starting transfers between devices  36.4 us (13%)
  between operations  15.5 us (5%)
  matrix products  13.1 us (5%)
  local copies, waits for them, and re-layouts  7 us (2%)
  other arithmetic  5.58 us (2%)
    all_gather x1, waiting for transfers between devices, shards(): lax.all_gather(out_weight, 'req', axis=1, tiled=True)  91.7 us
    psum x1, waiting for transfers between devices, shards(): lax.psum(partial_value.astype(jnp.bfloat16), 'tp').astype(jnp.float32)  72.7 us
    ppermute x4, waiting for transfers between devices, tracks_serve(): wide_out = lax.ppermute(y_new[-1], comm_axis, kept_rows)  26.1 us
    all_to_all x1, starting transfers between devices, shards(): lax.all_to_all(outgoing.reshape(requests, capacity, feature_width), 'req'...  14.2 us
    ppermute x3, starting transfers between devices, tracks_serve(): q_next = lax.ppermute(new[-1], comm_axis, all_blocks)  13.7 us
    all_gather x1, waiting for transfers between devices, shards(): lax.all_gather(qkv_weight, 'req', axis=0, tiled=True)  10.8 us
    ppermute x4, starting transfers between devices, tracks_serve(): wide_out = lax.ppermute(y_new[-1], comm_axis, kept_rows)  8.41 us
    dot_general x1, matrix products, shards(): jnp.dot(normed, lax.all_gather(qkv_weight, 'req', axis=0, tiled=True), pr...  6.69 us
  transfers between devices with their start and end apart: 11, of which 9 were waited for; matrix products, arithmetic and copies ran while one was open for 4% of the time, Pallas kernels for 0%

profile of v1, /device:TPU:1, one launch (start us, length us, event | category | flops | bytes accessed | tf_op | source)
XLA Modules:
  0.0 287.8 jit_solution(23526176670924935)
XLA Ops:
  6.6 0.7 all-gather.3.cloned.1.call-update
  7.3 1.4 reshape.205
  8.7 0.6 reduce_sum.78
  9.3 91.7 %all-gather.3.cloned.1.call-done = bf16[512,4096]{0,1:T(8,128)(2,1)} async-done(((bf16[512,64]{0,1:T(8,128)(2,1)}), bf16[512,4096]{0,1:T(8,128)(2,1)}) %all-gather.3.cloned.1.call-update) | async-done | bytes 4194320 | tf_op jit(solution)/shard_map/all_gather | solution.py:97
  101.1 4.7 %convolution_convert_fusion = bf16[128,4096]{1,0:T(8,128)(2,1)} fusion(bf16[512,4096]{0,1:T(8,128)(2,1)} %all-gather.3.cloned.1.call-done, f32[128,512]{1,0:T(8,128)S(1)} %reduce_sum.78), kind=kOutput, calls=%fused_computation.5 | convolution fusion | flops 537526272 | bytes 5505024 | tf_op jit(solution)/shard_map/dot_general | solution.py:95
  105.8 0.7 all-gather.5.cloned.1.call-update
  107.3 0.6 reduce_sum.77
  108.0 0.7 fusion.39
  108.8 72.7 %all-reduce.2.cloned.1.call-done = bf16[128,4096]{1,0:T(8,128)(2,1)} async-done(((bf16[128,4096]{1,0:T(8,128)(2,1)}), bf16[128,4096]{1,0:T(8,128)(2,1)}) %all-reduce.2.cloned.1.call-update) | async-done | bytes 1048592 | tf_op jit(solution)/shard_map/psum | solution.py:100
  181.5 1.1 convolution_convert_fusion.1
  182.6 0.7 reshape.199
  183.3 14.2 %all-to-all-start = ((bf16[64,2,512]{2,1,0:T(2,128)(2,1)}), bf16[64,2,512]{2,1,0:T(2,128)(2,1)S(1)}, u32[]{:S(2)}, u32[]{:S(2)}) async-start(bf16[64,2,512]{2,1,0:T(2,128)(2,1)} %reshape.199), calls=%async_computation | async-start | bytes 262144 | tf_op jit(solution)/shard_map/all_to_all | solution.py:120
  199.4 0.6 fusion.38
  200.0 1.2 fusion.31
  201.3 6.6 %all-to-all-done = bf16[64,2,512]{2,1,0:T(2,128)(2,1)S(1)} async-done(((bf16[64,2,512]{2,1,0:T(2,128)(2,1)}), bf16[64,2,512]{2,1,0:T(2,128)(2,1)S(1)}, u32[]{:S(2)}, u32[]{:S(2)}) %all-to-all-start) | async-done | bytes 131104 | tf_op jit(solution)/shard_map/all_to_all | solution.py:120
  208.6 2.7 collective-permute-start
  211.3 10.8 %collective-permute-done = bf16[384,512]{1,0:T(8,128)(2,1)S(1)} collective-permute-done((bf16[384,512]{1,0:T(8,128)(2,1)S(1)}, bf16[384,512]{1,0:T(8,128)(2,1)S(1)}, u32[]{:S(2)}, u32[]{:S(2)}) %collective-permute-start) | collective-permute-done | bytes 393248 | tf_op jit(solution)/shard_map/ppermute | solution.py:18
  222.1 1.9 collective-permute-start.1
  224.0 4.6 %collective-permute-start.4 = (bf16[384,512]{1,0:T(8,128)(2,1)S(1)}, bf16[384,512]{1,0:T(8,128)(2,1)S(1)}, u32[]{:S(2)}, u32[]{:S(2)}) collective-permute-start(bf16[384,512]{1,0:T(8,128)(2,1)S(1)} %fusion.8), channel_id=1, source_target_pairs={{0,7},{1,0},{2,1},{3,2},{4,3},{5,4},{6,5},{7,6},{8,15},{9,8},{10,9... | collective-permute-start | bytes 1179656 | tf_op jit(solution)/shard_map/ppermute | solution.py:21
  228.6 6.1 %collective-permute-done.1 = bf16[384,512]{1,0:T(8,128)(2,1)S(1)} collective-permute-done((bf16[384,512]{1,0:T(8,128)(2,1)S(1)}, bf16[384,512]{1,0:T(8,128)(2,1)S(1)}, u32[]{:S(2)}, u32[]{:S(2)}) %collective-permute-start.1) | collective-permute-done | bytes 393248 | tf_op jit(solution)/shard_map/ppermute | solution.py:18
  234.7 1.9 collective-permute-start.2
  236.6 4.6 %collective-permute-start.5 = (bf16[384,512]{1,0:T(8,128)(2,1)S(1)}, bf16[384,512]{1,0:T(8,128)(2,1)S(1)}, u32[]{:S(2)}, u32[]{:S(2)}) collective-permute-start(bf16[384,512]{1,0:T(8,128)(2,1)S(1)} %collective-permute-done.4), channel_id=1, source_target_pairs={{0,7},{1,0},{2,1},{3,2},{4,3},{5,4},{6,5},{7,6},{8,15},{9,8},{10,9... | collective-permute-start | bytes 1179656 | tf_op jit(solution)/shard_map/ppermute | solution.py:21
  241.2 5.3 %collective-permute-done.2 = bf16[384,512]{1,0:T(8,128)(2,1)S(1)} collective-permute-done((bf16[384,512]{1,0:T(8,128)(2,1)S(1)}, bf16[384,512]{1,0:T(8,128)(2,1)S(1)}, u32[]{:S(2)}, u32[]{:S(2)}) %collective-permute-start.2) | collective-permute-done | bytes 393248 | tf_op jit(solution)/shard_map/ppermute | solution.py:18
  246.4 1.9 collective-permute-start.3
  248.8 4.6 %collective-permute-start.6 = (bf16[384,512]{1,0:T(8,128)(2,1)S(1)}, bf16[384,512]{1,0:T(8,128)(2,1)S(1)}, u32[]{:S(2)}, u32[]{:S(2)}) collective-permute-start(bf16[384,512]{1,0:T(8,128)(2,1)S(1)} %collective-permute-done.5), channel_id=1, source_target_pairs={{0,7},{1,0},{2,1},{3,2},{4,3},{5,4},{6,5},{7,6},{8,15},{9,8},{10,9... | collective-permute-start | bytes 1179656 | tf_op jit(solution)/shard_map/ppermute | solution.py:21
  253.4 4.0 %collective-permute-done.3 = bf16[384,512]{1,0:T(8,128)(2,1)S(1)} collective-permute-done((bf16[384,512]{1,0:T(8,128)(2,1)S(1)}, bf16[384,512]{1,0:T(8,128)(2,1)S(1)}, u32[]{:S(2)}, u32[]{:S(2)}) %collective-permute-start.3) | collective-permute-done | bytes 393248 | tf_op jit(solution)/shard_map/ppermute | solution.py:18
  257.7 0.9 collective-permute-done.6
  259.1 2.7 copy-done.1
  261.8 0.7 fusion
  262.5 10.8 %all-gather.5.cloned.1.call-done = bf16[4096,768]{1,0:T(8,128)(2,1)} async-done(((bf16[64,768]{1,0:T(8,128)(2,1)}), bf16[4096,768]{1,0:T(8,128)(2,1)}) %all-gather.5.cloned.1.call-update) | async-done | bytes 6291472 | tf_op jit(solution)/shard_map/all_gather | solution.py:156
  273.3 6.7 %fusion.3 = f32[384,768]{0,1:T(8,128)S(1)} fusion(bf16[4096,768]{1,0:T(8,128)(2,1)} %all-gather.5.cloned.1.call-done, f32[4096]{0:T(1024)S(1)} %copy-done.4, f32[384]{0:T(512)S(1)} %add_rsqrt_fusion, bf16[384,8192]{1,0:T(8,128)(2,1)} %copy-done.1, s32[]{:T(128)S(6)} %select_n.71), kind=kOutput, calls=%fused_computation.6 | convolution fusion | flops 2422210560 | bytes 10634756 | tf_op jit(solution)/shard_map/dot_general | solution.py:154
  280.2 1.1 copy.18
  (55 shorter events, 3.1 us)
Async XLA Ops:
  6.5 201.7 %copy-start = (bf16[1,256,512]{2,1,0:T(8,128)(2,1)S(1)}, bf16[1,256,512]{2,1,0:T(8,128)(2,1)}, u32[]{:S(2)}) copy-start(bf16[1,256,512]{2,1,0:T(8,128)(2,1)} %param.15) | copy-start | bytes 786436
  6.5 100.0 %copy-start.5 = (s32[128,2]{0,1:T(2,128)S(1)}, s32[128,2]{0,1:T(2,128)}, u32[]{:S(2)}) copy-start(s32[128,2]{0,1:T(2,128)} %param.18) | copy-start | bytes 3076
  6.5 100.0 %copy-start.6 = (s32[128]{0:T(128)S(1)}, s32[128]{0:T(128)}, u32[]{:S(2)}) copy-start(s32[128]{0:T(128)} %param.19) | copy-start | bytes 1540
  6.5 100.4 %copy-start.2 = (bf16[512,512]{1,0:T(8,128)(2,1)S(1)}, bf16[512,512]{1,0:T(8,128)(2,1)}, u32[]{:S(2)}) copy-start(bf16[512,512]{1,0:T(8,128)(2,1)} %param.12) | copy-start | bytes 1572868
  6.5 94.5 %all-gather.3.cloned.1.call-start = ((), (), s32[]{:S(2)}) async-start(), calls=%async_computation.1 | async-start | bytes 4259840 | tf_op jit(solution)/shard_map/all_gather | solution.py:97
  7.3 174.2 %copy-start.3 = (f32[512]{0:T(512)S(1)}, f32[512]{0:T(512)}, u32[]{:S(2)}) copy-start(f32[512]{0:T(512)} %param.14) | copy-start | bytes 6148
  7.3 174.2 %all-reduce.2.cloned.1.call-start = ((), (), s32[]{:S(2)}) async-start(), calls=%async_computation.2 | async-start | bytes 2097152 | tf_op jit(solution)/shard_map/psum | solution.py:100
  105.8 167.5 %all-gather.5.cloned.1.call-start = ((), (), s32[]{:S(2)}) async-start(), calls=%async_computation.3 | async-start | bytes 6389760 | tf_op jit(solution)/shard_map/all_gather | solution.py:156
  183.3 24.5 %all-to-all-start = ((bf16[64,2,512]{2,1,0:T(2,128)(2,1)}), bf16[64,2,512]{2,1,0:T(2,128)(2,1)S(1)}, u32[]{:S(2)}, u32[]{:S(2)}) async-start(bf16[64,2,512]{2,1,0:T(2,128)(2,1)} %reshape.199), calls=%async_computation | async-start | bytes 262144 | tf_op jit(solution)/shard_map/all_to_all | solution.py:120
  208.6 13.5 %collective-permute-start = (bf16[384,512]{1,0:T(8,128)(2,1)S(1)}, bf16[384,512]{1,0:T(8,128)(2,1)S(1)}, u32[]{:S(2)}, u32[]{:S(2)}) collective-permute-start(bf16[384,512]{1,0:T(8,128)(2,1)S(1)} %fusion.8), channel_id=1, source_target_pairs={{0,1},{1,2},{2,3},{3,4},{4,5},{5,6},{6,7},{7,0},{8,9},{9,10},{10,1... | collective-permute-start | bytes 1179656 | tf_op jit(solution)/shard_map/ppermute | solution.py:18
  222.1 12.6 %collective-permute-start.1 = (bf16[384,512]{1,0:T(8,128)(2,1)S(1)}, bf16[384,512]{1,0:T(8,128)(2,1)S(1)}, u32[]{:S(2)}, u32[]{:S(2)}) collective-permute-start(bf16[384,512]{1,0:T(8,128)(2,1)S(1)} %collective-permute-done), channel_id=1, source_target_pairs={{0,1},{1,2},{2,3},{3,4},{4,5},{5,6},{6,7},{7,0},{8,9},{9,10},{10,1... | collective-permute-start | bytes 1179656 | tf_op jit(solution)/shard_map/ppermute | solution.py:18
  224.0 12.6 %collective-permute-start.4 = (bf16[384,512]{1,0:T(8,128)(2,1)S(1)}, bf16[384,512]{1,0:T(8,128)(2,1)S(1)}, u32[]{:S(2)}, u32[]{:S(2)}) collective-permute-start(bf16[384,512]{1,0:T(8,128)(2,1)S(1)} %fusion.8), channel_id=1, source_target_pairs={{0,7},{1,0},{2,1},{3,2},{4,3},{5,4},{6,5},{7,6},{8,15},{9,8},{10,9... | collective-permute-start | bytes 1179656 | tf_op jit(solution)/shard_map/ppermute | solution.py:21
  234.7 11.8 %collective-permute-start.2 = (bf16[384,512]{1,0:T(8,128)(2,1)S(1)}, bf16[384,512]{1,0:T(8,128)(2,1)S(1)}, u32[]{:S(2)}, u32[]{:S(2)}) collective-permute-start(bf16[384,512]{1,0:T(8,128)(2,1)S(1)} %collective-permute-done.1), channel_id=1, source_target_pairs={{0,1},{1,2},{2,3},{3,4},{4,5},{5,6},{6,7},{7,0},{8,9},{9,10},{10,1... | collective-permute-start | bytes 1179656 | tf_op jit(solution)/shard_map/ppermute | solution.py:18
  236.6 12.2 %collective-permute-start.5 = (bf16[384,512]{1,0:T(8,128)(2,1)S(1)}, bf16[384,512]{1,0:T(8,128)(2,1)S(1)}, u32[]{:S(2)}, u32[]{:S(2)}) collective-permute-start(bf16[384,512]{1,0:T(8,128)(2,1)S(1)} %collective-permute-done.4), channel_id=1, source_target_pairs={{0,7},{1,0},{2,1},{3,2},{4,3},{5,4},{6,5},{7,6},{8,15},{9,8},{10,9... | collective-permute-start | bytes 1179656 | tf_op jit(solution)/shard_map/ppermute | solution.py:21
  246.4 10.9 %collective-permute-start.3 = (bf16[384,512]{1,0:T(8,128)(2,1)S(1)}, bf16[384,512]{1,0:T(8,128)(2,1)S(1)}, u32[]{:S(2)}, u32[]{:S(2)}) collective-permute-start(bf16[384,512]{1,0:T(8,128)(2,1)S(1)} %collective-permute-done.2), channel_id=1, source_target_pairs={{0,1},{1,2},{2,3},{3,4},{4,5},{5,6},{6,7},{7,0},{8,9},{9,10},{10,1... | collective-permute-start | bytes 1179656 | tf_op jit(solution)/shard_map/ppermute | solution.py:18
  248.8 9.8 %collective-permute-start.6 = (bf16[384,512]{1,0:T(8,128)(2,1)S(1)}, bf16[384,512]{1,0:T(8,128)(2,1)S(1)}, u32[]{:S(2)}, u32[]{:S(2)}) collective-permute-start(bf16[384,512]{1,0:T(8,128)(2,1)S(1)} %collective-permute-done.5), channel_id=1, source_target_pairs={{0,7},{1,0},{2,1},{3,2},{4,3},{5,4},{6,5},{7,6},{8,15},{9,8},{10,9... | collective-permute-start | bytes 1179656 | tf_op jit(solution)/shard_map/ppermute | solution.py:21
  257.6 15.7 %copy-start.4 = (f32[4096]{0:T(1024)S(1)}, f32[4096]{0:T(1024)}, u32[]{:S(2)}) copy-start(f32[4096]{0:T(1024)} %param.20) | copy-start | bytes 49156
  259.1 2.7 copy-start.1
Sparse Core Ops, SparseCore 0:
  10.7 90.2 all-gather.2
  105.9 75.5 all-reduce.1
  184.8 88.4 all-gather.4
